TPU v7x, 256 devices: a whole 4x4x8 slice. The times are simulated.
256 devices in a mesh: row: 32 (over z, x), col: 8 (over y, core).
Axes of the slice: x: 4, y: 4, z: 8, core: 2. Of those that a mesh axis runs over, the one named last changes fastest.
Arguments:
- kernel: float32 [1, 32, 256, 4, 8, 256], P(None, 'row', None, None, 'col'), as said below
Outputs:
- factor: float32 [1, 32, 256, 4, 8, 256], P(None, 'row', None, None, 'col')
Inputs may be any that keep to these rules, and one draw needn't show every extreme that they name: kernel is a symmetric positive definite matrix.
All inputs are finite; a program needn't handle non-finite values.
Results may differ from a plain program's by a relative error of at most 0.0003.
Values sent between devices are 32-bit elements; how exact they have to be, the bound alone decides.
No kernel may reach another device: no remote copies, remote signals or barrier semaphores. Data moves between devices by JAX's collectives and lax.ppermute only.
A program may use at most 64 MiB of HBM per device.

v0:
```python
import jax
import jax.numpy as jnp
from jax import lax
from jax.sharding import PartitionSpec as P

PANELS = 2


def spread_2(x, axis, root):
    mine = lax.axis_index(axis) == root
    return lax.psum(jnp.where(mine, x, jnp.zeros_like(x)), axis)


def solve_panel(diag_factor, blocks, block_index, k):
    count, block_size, _ = blocks.shape
    flat_rows = blocks.reshape(count * block_size, block_size)
    solved = jax.scipy.linalg.solve_triangular(diag_factor, flat_rows.T, lower=True).T.reshape(
        count, block_size, block_size
    )
    marks = block_index[:, None, None]
    return jnp.where(marks > k, solved, jnp.where(marks == k, diag_factor[None], 0.0))


def spread_panel(panel_blocks, col_id, row_devs, col_devs):
    spread = row_devs // col_devs
    gathered_parts = [spread_2(panel_blocks, "row", col_id + m * col_devs) for m in range(spread)]
    stacked_parts = jnp.stack(gathered_parts, axis=1)
    count, _, block_size, _ = stacked_parts.shape
    return stacked_parts.reshape(count * spread, block_size, block_size)


def outer_update(left_factor, right_factor):
    rows_local, block_size, _ = left_factor.shape
    cols_local = right_factor.shape[0]
    update_term = lax.dot_general(
        left_factor.reshape(rows_local * block_size, block_size),
        right_factor.reshape(cols_local * block_size, block_size),
        (((1,), (1,)), ((), ())),
        precision=lax.Precision.HIGHEST,
    )
    return update_term.reshape(rows_local, block_size, cols_local, block_size)


def apply_step(tiles, update_term, row_blocks, col_blocks, solved_rows, k):
    zero_mask = (row_blocks[:, None, None, None] == k) & (col_blocks[None, None, :, None] > k)
    panel_mask = col_blocks[None, None, :, None] == k
    return jnp.where(
        panel_mask, solved_rows[:, :, None, :], jnp.where(zero_mask, 0.0, tiles - update_term)
    )


def shards(kernel):
    rows_local, _, block_size, cols_local, _, _ = kernel.shape
    row_devs = lax.axis_size("row")
    col_devs = lax.axis_size("col")
    row_id = lax.axis_index("row")
    col_id = lax.axis_index("col")
    matrix_tiles = kernel.reshape(rows_local, block_size, cols_local, block_size)
    row_blocks = jnp.arange(rows_local, dtype=jnp.int32) * row_devs + row_id
    col_blocks = jnp.arange(cols_local, dtype=jnp.int32) * col_devs + col_id
    column = matrix_tiles[:, :, 0, :]
    for k in range(PANELS):
        owner_row = k % row_devs
        owner_col = k % col_devs
        local_row = k // row_devs
        next_col = (k + 1) // col_devs
        is_owner = col_id == owner_col
        pivot_block = jnp.where(is_owner, column[local_row], jnp.eye(block_size, dtype=jnp.float32))
        pivot_block = spread_2(pivot_block, "row", owner_row)
        diag_factor = jnp.linalg.cholesky(pivot_block)
        solved_rows = solve_panel(diag_factor, column, row_blocks, k)
        solved_rows = spread_2(solved_rows, "col", owner_col)
        column_factor = spread_panel(solved_rows, col_id, row_devs, col_devs)
        left_factor = jnp.where(row_blocks[:, None, None] > k, solved_rows, 0.0)
        right_factor = jnp.where(col_blocks[:, None, None] > k, column_factor, 0.0)
        matrix_tiles = apply_step(
            matrix_tiles,
            outer_update(left_factor, right_factor),
            row_blocks,
            col_blocks,
            solved_rows,
            k,
        )
        column = matrix_tiles[:, :, next_col, :]
    return matrix_tiles.reshape(kernel.shape)


def solution(mesh):
    in_specs = (P(None, "row", None, None, "col", None),)
    out_specs = P(None, "row", None, None, "col", None)
    return jax.shard_map(shards, mesh=mesh, in_specs=in_specs, out_specs=out_specs, check_vma=False)
```

profile of v0, /device:TPU:26, one launch (start us, length us, event | category | flops | bytes accessed | tf_op | source)
XLA Modules:
  0.0 876.5 jit_solution(10389183939746000269)
XLA Ops:
  6.5 2.3 copy.2
  8.9 0.7 fusion.21
  9.7 148.1 %all-reduce.10.cloned.1.call-done = f32[256,256]{0,1:T(8,128)} async-done(((f32[256,256]{0,1:T(8,128)}), f32[256,256]{0,1:T(8,128)}) %all-reduce.10.cloned.1.call-update) | async-done | bytes 262160 | tf_op jit(solution)/shard_map/psum | solution.py:11
  157.8 1.1 copy.3
  159.0 11.7 %cholesky.130 = f32[128,128]{1,0:T(8,128)S(1)} custom-call(f32[128,128]{1,0:T(8,128)S(1)} %cholesky.194), custom_call_target="Cholesky" | custom-call | tf_op jit(solution)/shard_map/jit(cholesky)/cholesky | solution.py:70
  170.8 9.8 %custom-call.13 = f32[1,128,128]{1,2,0:T(8,128)S(1)} custom-call(f32[1,128,128]{2,1,0:T(8,128)S(1)} %get-tuple-element.70), custom_call_target="InvertDiagBlocksLowerTriangular" | custom-call | tf_op jit(solution)/shard_map/jit(cholesky)/cholesky | solution.py:70
  181.1 11.7 %cholesky.147 = f32[128,128]{1,0:T(8,128)S(1)} custom-call(f32[128,128]{1,0:T(8,128)S(1)} %convolution_subtract_fusion.5), custom_call_target="Cholesky" | custom-call | tf_op jit(solution)/shard_map/jit(cholesky)/cholesky | solution.py:70
  195.4 4.5 while.4
  196.2 1.4 dynamic-slice.12
  198.3 1.4 dynamic-slice.12
  199.9 19.7 %custom-call.14 = f32[2,128,128]{1,2,0:T(8,128)S(1)} custom-call(f32[2,128,128]{2,1,0:T(8,128)S(1)} %get-tuple-element.21), custom_call_target="InvertDiagBlocksLowerTriangular" | custom-call | tf_op jit(solution)/shard_map/jit(_solve_triangular)/triangular_solve | solution.py:17
  220.5 0.8 fusion.25
  221.4 61.5 %all-reduce.12.cloned.1.call-done = f32[1,256,256]{1,2,0:T(8,128)} async-done(((f32[1,256,256]{1,2,0:T(8,128)}), f32[1,256,256]{1,2,0:T(8,128)}) %all-reduce.12.cloned.1.call-update) | async-done | bytes 262160 | tf_op jit(solution)/shard_map/psum | solution.py:11
  282.9 1.9 broadcast_select_fusion.7
  285.0 152.6 %all-reduce.20.cloned.1.call-done = (f32[1,256,256]{1,2,0:T(8,128)}, f32[1,256,256]{1,2,0:T(8,128)}, f32[1,256,256]{1,2,0:T(8,128)}, f32[1,256,256]{1,2,0:T(8,128)}) async-done(((f32[1,256,256]{1,2,0:T(8,128)}, f32[1,256,256]{1,2,0:T(8,128)}, f32[1,256,256]{1,2,0:T(8,128)}, f32[1,256,256]{1,2,0:T(8,128)}), (f32[1,256,256]{1,2,0:T(8,128)}, f32[1,256,256]{1,2,0:T(8,128)}, f32[1,256,256]{1,2,0:T(8,128)}, ...) | async-done | bytes 1048592 | tf_op jit(solution)/shard_map/psum | solution.py:11
  437.6 3.2 fusion.4
  440.7 0.7 fusion.22
  441.6 142.8 %all-reduce.14.cloned.1.call-done = f32[256,256]{0,1:T(8,128)} async-done(((f32[256,256]{0,1:T(8,128)}), f32[256,256]{0,1:T(8,128)}) %all-reduce.14.cloned.1.call-update) | async-done | bytes 262160 | tf_op jit(solution)/shard_map/psum | solution.py:11
  584.4 1.1 copy.12
  585.6 11.7 %cholesky.164 = f32[128,128]{1,0:T(8,128)S(1)} custom-call(f32[128,128]{1,0:T(8,128)S(1)} %cholesky.197), custom_call_target="Cholesky" | custom-call | tf_op jit(solution)/shard_map/jit(cholesky)/cholesky | solution.py:70
  597.4 9.8 %custom-call.15 = f32[1,128,128]{1,2,0:T(8,128)S(1)} custom-call(f32[1,128,128]{2,1,0:T(8,128)S(1)} %get-tuple-element.68), custom_call_target="InvertDiagBlocksLowerTriangular" | custom-call | tf_op jit(solution)/shard_map/jit(cholesky)/cholesky | solution.py:70
  607.7 11.7 %cholesky.181 = f32[128,128]{1,0:T(8,128)S(1)} custom-call(f32[128,128]{1,0:T(8,128)S(1)} %convolution_subtract_fusion.4), custom_call_target="Cholesky" | custom-call | tf_op jit(solution)/shard_map/jit(cholesky)/cholesky | solution.py:70
  622.5 4.6 while.5
  623.4 1.4 dynamic-slice.14
  625.6 1.4 dynamic-slice.14
  627.1 19.7 %custom-call.16 = f32[2,128,128]{1,2,0:T(8,128)S(1)} custom-call(f32[2,128,128]{2,1,0:T(8,128)S(1)} %get-tuple-element.22), custom_call_target="InvertDiagBlocksLowerTriangular" | custom-call | tf_op jit(solution)/shard_map/jit(_solve_triangular)/triangular_solve | solution.py:17
  647.8 0.8 fusion.28
  648.6 61.5 %all-reduce.16.cloned.1.call-done = f32[1,256,256]{1,2,0:T(8,128)} async-done(((f32[1,256,256]{1,2,0:T(8,128)}), f32[1,256,256]{1,2,0:T(8,128)}) %all-reduce.16.cloned.1.call-update) | async-done | bytes 262160 | tf_op jit(solution)/shard_map/psum | solution.py:11
  710.1 1.9 broadcast_select_fusion.3
  712.1 152.5 %all-reduce.18.cloned.1.call-done = (f32[1,256,256]{1,2,0:T(8,128)}, f32[1,256,256]{1,2,0:T(8,128)}, f32[1,256,256]{1,2,0:T(8,128)}, f32[1,256,256]{1,2,0:T(8,128)}) async-done(((f32[1,256,256]{1,2,0:T(8,128)}, f32[1,256,256]{1,2,0:T(8,128)}, f32[1,256,256]{1,2,0:T(8,128)}, f32[1,256,256]{1,2,0:T(8,128)}), (f32[1,256,256]{1,2,0:T(8,128)}, f32[1,256,256]{1,2,0:T(8,128)}, f32[1,256,256]{1,2,0:T(8,128)}, ...) | async-done | bytes 1048592 | tf_op jit(solution)/shard_map/psum | solution.py:11
  864.6 3.2 fusion.2
  867.8 1.9 copy.20
  (81 shorter events, 9.1 us)
Async XLA Ops:
  6.5 151.3 %all-reduce.10.cloned.1.call-start = ((), (), s32[]{:S(2)}) async-start(), calls=%async_computation | async-start | bytes 524288 | tf_op jit(solution)/shard_map/psum | solution.py:11
  9.7 273.3 %all-reduce.12.cloned.1.call-start = ((), (), s32[]{:S(2)}) async-start(), calls=%async_computation.1 | async-start | bytes 524288 | tf_op jit(solution)/shard_map/psum | solution.py:11
  157.8 1.2 copy-start
  221.3 216.2 %all-reduce.20.cloned.1.call-start = ((), (), s32[]{:S(2)}) async-start(), calls=%async_computation.5 | async-start | bytes 2097152 | tf_op jit(solution)/shard_map/psum | solution.py:11
  284.8 152.7 %copy-start.2 = (f32[1,256,256]{1,2,0:T(8,128)S(1)}, f32[1,256,256]{1,2,0:T(8,128)}, u32[]{:S(2)}) copy-start(f32[1,256,256]{1,2,0:T(8,128)} %all-reduce.12.cloned.1.call-done) | copy-start | bytes 786436
  284.9 299.5 %all-reduce.14.cloned.1.call-start = ((), (), s32[]{:S(2)}) async-start(), calls=%async_computation.2 | async-start | bytes 524288 | tf_op jit(solution)/shard_map/psum | solution.py:11
  441.5 268.6 %all-reduce.16.cloned.1.call-start = ((), (), s32[]{:S(2)}) async-start(), calls=%async_computation.3 | async-start | bytes 524288 | tf_op jit(solution)/shard_map/psum | solution.py:11
  584.4 1.2 copy-start.1
  648.5 216.1 %all-reduce.18.cloned.1.call-start = ((), (), s32[]{:S(2)}) async-start(), calls=%async_computation.4 | async-start | bytes 2097152 | tf_op jit(solution)/shard_map/psum | solution.py:11
  712.1 152.6 %copy-start.3 = (f32[1,256,256]{1,2,0:T(8,128)S(1)}, f32[1,256,256]{1,2,0:T(8,128)}, u32[]{:S(2)}) copy-start(f32[1,256,256]{1,2,0:T(8,128)} %all-reduce.16.cloned.1.call-done) | copy-start | bytes 786436
Sparse Core Ops, SparseCore 0:
  10.8 146.9 all-reduce.9
  221.4 61.4 all-reduce.11
  286.8 150.7 all-reduce.19
  441.6 142.7 all-reduce.13
  648.7 61.4 all-reduce.15
  713.8 150.7 all-reduce.17
where the time goes:
time: 878 us; the launch traced here: 877 us
  waiting for transfers between devices  719 us (82%)
  other arithmetic  115 us (13%)
  between operations  16.6 us (2%)
  local copies, waits for them, and re-layouts  15.8 us (2%)
  matrix products  9.12 us (1%)
    psum x6, waiting for transfers between devices, spread_2(): return lax.psum(jnp.where(mine, x, jnp.zeros_like(x)), axis)  719 us
    another operation x13, other arithmetic, shards(): diag_factor = jnp.linalg.cholesky(pivot_block)  68.7 us
    another operation x5, other arithmetic, solve_panel(): jax.scipy.linalg.solve_triangular(diag_factor, flat_rows.T, lower=True)  39.4 us
  transfers between devices with their start and end apart: 6, of which 6 were waited for; matrix products, arithmetic and copies ran while one was open for 0% of the time, Pallas kernels for 0%

commit v1 on v0

v1 whole, which is shorter than its diff:
```python
import jax
import jax.numpy as jnp
from jax import lax
from jax.scipy.linalg import solve_triangular
from jax.sharding import PartitionSpec as P

PANELS = 2
HIGHEST = lax.Precision.HIGHEST


def dot(a, b):
    return jnp.dot(a, b, precision=HIGHEST)


def lead_rows_to_all(tiles):
    block_size, cols_local, _ = tiles.shape
    row_devs = lax.axis_size("row")
    piece = block_size // row_devs
    send = tiles.reshape(row_devs, piece, cols_local, block_size)
    spread = lax.all_to_all(send, "row", 0, 0)[:PANELS]
    send = jnp.broadcast_to(spread[None], (row_devs,) + spread.shape)
    gathered = lax.all_to_all(send, "row", 0, 0)
    return gathered.transpose(1, 0, 2, 3, 4).reshape(PANELS, block_size, cols_local, block_size)


def from_lead_cols(payload):
    col_devs = lax.axis_size("col")
    col_id = lax.axis_index("col")
    have = PANELS
    while have < col_devs:
        pairs = [(i, i + have) for i in range(have) if i + have < col_devs]
        got = lax.ppermute(payload, "col", pairs)
        fresh = (col_id >= have) & (col_id < 2 * have)
        payload = jnp.where(fresh, got, payload)
        have *= 2
    return payload


def shards(kernel):
    _, _, block_size, cols_local, _, _ = kernel.shape
    row_id = lax.axis_index("row")
    col_id = lax.axis_index("col")
    lead = PANELS * block_size
    tiles = kernel.reshape(block_size, cols_local, block_size)

    lead_block = lead_rows_to_all(tiles)

    mine = jnp.stack([tiles[:, 0, :], lead_block[0, :, 0, :], lead_block[1, :, 0, :]])
    other = lax.ppermute(mine, "col", [(0, 1), (1, 0)])
    first, second = jnp.where(col_id == 0, mine, other), jnp.where(col_id == 0, other, mine)
    payload = jnp.stack([first[0], second[0], first[1], first[2], second[2]])
    row_0, row_1, m00, m10, m11 = from_lead_cols(payload)

    lead_matrix = jnp.concatenate(
        [jnp.concatenate([m00, m10.T], axis=1), jnp.concatenate([m10, m11], axis=1)], axis=0
    )
    factor = jnp.linalg.cholesky(lead_matrix)
    inverse = solve_triangular(factor, jnp.eye(lead, dtype=jnp.float32), lower=True)

    right = dot(inverse, lead_block.reshape(lead, cols_local * block_size))
    left = lax.dot_general(
        jnp.concatenate([row_0, row_1], axis=1), inverse, (((1,), (1,)), ((), ())), precision=HIGHEST
    )
    left = jnp.where(
        row_id == 0,
        factor[:block_size],
        jnp.where(row_id == 1, factor[block_size:], left),
    )
    update = dot(left, right).reshape(block_size, cols_local, block_size)
    trailing = jnp.where(row_id >= PANELS, tiles - update, 0.0)
    panel = jnp.where(col_id == 0, left[:, :block_size], left[:, block_size:])
    first_col = jnp.where(col_id < PANELS, panel, trailing[:, 0, :])
    out = trailing.at[:, 0, :].set(first_col)
    return out.reshape(kernel.shape)


def solution(mesh):
    in_specs = (P(None, "row", None, None, "col", None),)
    out_specs = P(None, "row", None, None, "col", None)
    return jax.shard_map(shards, mesh=mesh, in_specs=in_specs, out_specs=out_specs, check_vma=False)
```

time: 878 us -> 374 us (0.43)
  waiting for transfers between devices: 719 us -> 105 us
  blocking collectives: 0 us -> 39.5 us
  local copies, waits for them, and re-layouts: 15.8 us -> 46.8 us
  other arithmetic: 115 us -> 144 us
  between operations: 16.6 us -> 3.23 us
  matrix products: 9.12 us -> 20.1 us
  starting transfers between devices: 0.21 us -> 10.4 us
    psum x6 -> x0, waiting for transfers between devices: 719 us -> none  [spread_2(): return lax.psum(jnp.where(mine, x, jnp.zeros_like(x)), axis)]
    ppermute x0 -> x3, waiting for transfers between devices: none -> 59.2 us  [the longest x2 59.2 us: from_lead_cols(): got = lax.ppermute(payload, 'col', pairs)]
    all_to_all x0 -> x1, waiting for transfers between devices: none -> 45.4 us  [lead_rows_to_all(): gathered = lax.all_to_all(send, 'row', 0, 0)]
    all_to_all x0 -> x1, blocking collectives: none -> 39.5 us  [lead_rows_to_all(): spread = lax.all_to_all(send, 'row', 0, 0)[:PANELS]]
    another operation x18 -> x19, other arithmetic: 108 us -> 127 us  [the longest x14 81.1 us: shards(): factor = jnp.linalg.cholesky(lead_matrix)]
    another operation x37, local copies, waits for them, and re-layouts: 9.24 us -> 21.5 us  [the longest x23 8.6 us: solve_panel(): jax.scipy.linalg.solve_triangular(diag_factor, flat_rows.T, lower=True)]
    unnamed x9 -> x38, local copies, waits for them, and re-layouts: 2.36 us -> 13.4 us
    another operation x10 -> x13, matrix products: 2.8 us -> 13.6 us  [the longest x7 6.81 us: shards(): solve_triangular(factor, jnp.eye(lead, dtype=jnp.float32), lower=True)]
  transfers between devices with their start and end apart: 6 -> 4, of which waited for: 6 -> 2; matrix products, arithmetic and copies ran while one was open for 0% -> 2% of each run, Pallas kernels for 0% -> 0%
where the time goes in v1:
time: 374 us; the launch traced here: 369 us
  other arithmetic  144 us (39%)
  waiting for transfers between devices  105 us (28%)
  local copies, waits for them, and re-layouts  46.8 us (13%)
  blocking collectives  39.5 us (11%)
  matrix products  20.1 us (5%)
  starting transfers between devices  10.4 us (3%)
    another operation x14, other arithmetic, shards(): factor = jnp.linalg.cholesky(lead_matrix)  81.1 us
    ppermute x2, waiting for transfers between devices, from_lead_cols(): got = lax.ppermute(payload, 'col', pairs)  59.2 us
    all_to_all x1, waiting for transfers between devices, lead_rows_to_all(): gathered = lax.all_to_all(send, 'row', 0, 0)  45.4 us
    another operation x3, other arithmetic, shards(): solve_triangular(factor, jnp.eye(lead, dtype=jnp.float32), lower=True)  42.9 us
    all_to_all x1, blocking collectives, lead_rows_to_all(): spread = lax.all_to_all(send, 'row', 0, 0)[:PANELS]  39.5 us
    another operation x20, local copies, waits for them, and re-layouts  14.3 us
    unnamed x38, local copies, waits for them, and re-layouts  13.4 us
  transfers between devices with their start and end apart: 4, of which 2 were waited for; matrix products, arithmetic and copies ran while one was open for 2% of the time, Pallas kernels for 0%

profile of v1, /device:TPU:26, one launch (start us, length us, event | category | flops | bytes accessed | tf_op | source)
XLA Modules:
  0.0 368.6 jit_solution(1920474116517377297)
XLA Ops:
  1.7 39.5 %all_to_all.10 = f32[32,8,4,256]{3,1,2,0:T(8,128)S(1)} all-to-all(f32[32,8,4,256]{3,1,2,0:T(8,128)S(1)} %copy.40), channel_id=1, replica_groups=mesh['row'=32,'col'=8] {'row'}, dimensions={0} | all-to-all | bytes 2097152 | tf_op jit(solution)/shard_map/all_to_all | solution.py:20
  42.8 5.7 %all-to-all-start.1 = ((f32[32,2,8,4,256]{4,2,3,1,0:T(8,128)}), f32[32,2,8,4,256]{4,2,3,1,0:T(8,128)S(1)}, u32[]{:S(2)}, u32[]{:S(2)}) async-start(f32[32,2,8,4,256]{4,2,3,1,0:T(8,128)} %broadcast_in_dim.14), calls=%async_computation.1 | async-start | bytes 4194304 | tf_op jit(solution)/shard_map/all_to_all | solution.py:22
  48.5 2.1 copy.39
  51.6 45.4 %all-to-all-done.1 = f32[32,2,8,4,256]{4,2,3,1,0:T(8,128)S(1)} async-done(((f32[32,2,8,4,256]{4,2,3,1,0:T(8,128)}), f32[32,2,8,4,256]{4,2,3,1,0:T(8,128)S(1)}, u32[]{:S(2)}, u32[]{:S(2)}) %all-to-all-start.1) | async-done | bytes 2097184 | tf_op jit(solution)/shard_map/all_to_all | solution.py:22
  98.0 1.8 copy.66
  99.8 1.8 copy.67
  101.6 2.0 pad_maximum_fusion.2
  108.0 1.7 collective-permute-start.1
  109.7 2.4 broadcast_select_fusion.1
  117.0 59.2 %collective-permute-done.2 = f32[5,256,256]{1,2,0:T(8,128)} collective-permute-done((f32[5,256,256]{1,2,0:T(8,128)}, f32[5,256,256]{1,2,0:T(8,128)}, u32[]{:S(2)}, u32[]{:S(2)}) %collective-permute-start.2) | collective-permute-done | bytes 1310752 | tf_op jit(solution)/shard_map/ppermute | solution.py:32
  178.8 1.8 copy.68
  180.6 1.9 pad_maximum_fusion.5
  182.4 2.0 copy.45
  184.5 2.2 maximum_maximum_fusion
  186.7 2.5 copy.46
  191.9 11.7 %cholesky.104 = f32[128,128]{1,0:T(8,128)S(1)} custom-call(f32[128,128]{1,0:T(8,128)S(1)} %cholesky.266), custom_call_target="Cholesky" | custom-call | tf_op jit(solution)/shard_map/jit(cholesky)/cholesky | solution.py:57
  204.2 9.8 %custom-call.31 = f32[1,128,128]{1,2,0:T(8,128)S(1)} custom-call(f32[1,128,128]{2,1,0:T(8,128)S(1)} %get-tuple-element.66), custom_call_target="InvertDiagBlocksLowerTriangular" | custom-call | tf_op jit(solution)/shard_map/jit(cholesky)/cholesky | solution.py:57
  217.2 12.1 %cholesky.217 = f32[128,128]{1,0:T(8,128)S(1)} custom-call(f32[128,128]{1,0:T(8,128)S(1)} %cholesky.270), custom_call_target="Cholesky" | custom-call | tf_op jit(solution)/shard_map/jit(cholesky)/cholesky | solution.py:57
  232.4 11.3 %custom-call.32 = f32[1,128,128]{1,2,0:T(8,128)} custom-call(f32[1,128,128]{2,1,0:T(8,128)} %get-tuple-element.64), custom_call_target="InvertDiagBlocksLowerTriangular" | custom-call | tf_op jit(solution)/shard_map/jit(cholesky)/cholesky | solution.py:57
  247.5 11.7 %cholesky.238 = f32[128,128]{1,0:T(8,128)S(1)} custom-call(f32[128,128]{1,0:T(8,128)S(1)} %cholesky.275), custom_call_target="Cholesky" | custom-call | tf_op jit(solution)/shard_map/jit(cholesky)/cholesky | solution.py:57
  260.0 9.8 %custom-call.33 = f32[1,128,128]{1,2,0:T(8,128)S(1)} custom-call(f32[1,128,128]{2,1,0:T(8,128)S(1)} %get-tuple-element.62), custom_call_target="InvertDiagBlocksLowerTriangular" | custom-call | tf_op jit(solution)/shard_map/jit(cholesky)/cholesky | solution.py:57
  272.3 11.9 %cholesky.255 = f32[128,128]{1,0:T(8,128)S(1)} custom-call(f32[128,128]{1,0:T(8,128)S(1)} %convolution_subtract_fusion.5), custom_call_target="Cholesky" | custom-call | tf_op jit(solution)/shard_map/jit(cholesky)/cholesky | solution.py:57
  289.5 2.8 fusion.2
  292.4 14.4 %while.2 = (s32[]{:T(128)}, f32[512,512]{0,1:T(8,128)}, s32[4,2]{0,1:T(2,128)S(1)}, f32[4,128,128]{2,1,0:T(8,128)}, s32[]{:T(128)}) while((s32[]{:T(128)}, f32[512,512]{0,1:T(8,128)}, s32[4,2]{0,1:T(2,128)S(1)}, f32[4,128,128]{2,1,0:T(8,128)}, s32[]{:T(128)}) %tuple.39), condition=%wide.while_cond.1, body=%wide.while_body.1.sunk | while | flops 2 | bytes 393829 | solution.py:58
  293.0 2.2 dynamic-slice.15
  296.6 2.2 dynamic-slice.15
  300.2 2.2 dynamic-slice.15
  303.9 2.2 dynamic-slice.15
  306.7 40.1 %custom-call.34 = f32[4,128,128]{1,2,0:T(8,128)S(1)} custom-call(f32[4,128,128]{2,1,0:T(8,128)} %get-tuple-element.24), custom_call_target="InvertDiagBlocksLowerTriangular" | custom-call | tf_op jit(solution)/shard_map/jit(_solve_triangular)/triangular_solve | solution.py:58
  353.8 3.6 fusion.8
  359.3 1.9 fusion.46
  365.2 2.3 broadcast_select_fusion
  (113 shorter events, 55.3 us)
Async XLA Ops:
  42.8 5.7 %copy-start = (f32[1,1,256,4,1,256]{5,4,3,2,1,0:T(1,128)S(1)}, f32[1,1,256,4,1,256]{5,4,3,2,1,0:T(1,128)}, u32[]{:S(2)}) copy-start(f32[1,1,256,4,1,256]{5,4,3,2,1,0:T(1,128)} %param.3) | copy-start | bytes 3145732
  42.8 54.2 %all-to-all-start.1 = ((f32[32,2,8,4,256]{4,2,3,1,0:T(8,128)}), f32[32,2,8,4,256]{4,2,3,1,0:T(8,128)S(1)}, u32[]{:S(2)}, u32[]{:S(2)}) async-start(f32[32,2,8,4,256]{4,2,3,1,0:T(8,128)} %broadcast_in_dim.14), calls=%async_computation.1 | async-start | bytes 4194304 | tf_op jit(solution)/shard_map/all_to_all | solution.py:22
  103.6 1.6 collective-permute-start
  106.6 1.4 copy-start.2
  106.7 1.3 copy-start.5
  106.7 1.3 copy-start.6
  108.0 1.7 collective-permute-start.1
  112.2 64.0 %collective-permute-start.2 = (f32[5,256,256]{1,2,0:T(8,128)}, f32[5,256,256]{1,2,0:T(8,128)}, u32[]{:S(2)}, u32[]{:S(2)}) collective-permute-start(f32[5,256,256]{1,2,0:T(8,128)} %broadcast_select_fusion.1), channel_id=1, source_target_pairs={{0,4},{1,5},{2,6},{3,7},{8,12},{9,13},{10,14},{11,15},{16,20},{17,... | collective-permute-start | bytes 3932168 | tf_op jit(solution)/shard_map/ppermute | solution.py:32
  190.9 1.0 copy-start.4
  203.6 0.6 copy-start.11
  216.5 0.7 copy-start.9
  230.8 13.9 %copy-start.10 = (f32[384,128]{1,0:T(8,128)S(1)}, f32[384,128]{1,0:T(8,128)}, u32[]{:S(2)}) copy-start(f32[384,128]{1,0:T(8,128)} %copy-done.9) | copy-start | bytes 589828
  243.7 1.0 copy-start.12
  243.7 1.1 copy-start.15
  245.1 1.0 copy-start.1
  346.9 3.0 copy-start.3
  353.8 3.6 copy-start.8
  353.8 3.6 copy-start.13
  353.8 3.6 copy-start.14
  358.5 0.8 copy-start.7

commit v2 on v1

--- a/solution.py
+++ b/solution.py
@@ -36,6 +36,40 @@
     return payload
 
 
+def blocked_factor(matrix, step):
+    count = matrix.shape[0] // step
+    blocks = [[matrix[i * step:(i + 1) * step, j * step:(j + 1) * step] for j in range(count)] for i in range(count)]
+    eye = jnp.eye(step, dtype=jnp.float32)
+    low = [[None] * count for _ in range(count)]
+    inv_diag = []
+    for k in range(count):
+        diag = jnp.linalg.cholesky(blocks[k][k])
+        inv = solve_triangular(diag, eye, lower=True)
+        low[k][k] = diag
+        inv_diag.append(inv)
+        if k + 1 < count:
+            below = jnp.concatenate([blocks[i][k] for i in range(k + 1, count)], axis=0)
+            below = lax.dot_general(below, inv, (((1,), (1,)), ((), ())), precision=HIGHEST)
+            for i in range(k + 1, count):
+                low[i][k] = below[(i - k - 1) * step:(i - k) * step]
+            shrink = lax.dot_general(below, below, (((1,), (1,)), ((), ())), precision=HIGHEST)
+            for i in range(k + 1, count):
+                for j in range(k + 1, i + 1):
+                    blocks[i][j] = blocks[i][j] - shrink[(i - k - 1) * step:(i - k) * step, (j - k - 1) * step:(j - k) * step]
+    inverse = [[None] * count for _ in range(count)]
+    for j in range(count):
+        inverse[j][j] = inv_diag[j]
+        for i in range(j + 1, count):
+            acc = dot(low[i][j], inverse[j][j])
+            for k in range(j + 1, i):
+                acc = acc + dot(low[i][k], inverse[k][j])
+            inverse[i][j] = -dot(inv_diag[i], acc)
+    zero = jnp.zeros((step, step), jnp.float32)
+    factor = jnp.block([[low[i][j] if j <= i else zero for j in range(count)] for i in range(count)])
+    inverse = jnp.block([[inverse[i][j] if j <= i else zero for j in range(count)] for i in range(count)])
+    return factor, inverse
+
+
 def shards(kernel):
     _, _, block_size, cols_local, _, _ = kernel.shape
     row_id = lax.axis_index("row")
@@ -43,19 +77,22 @@
     lead = PANELS * block_size
     tiles = kernel.reshape(block_size, cols_local, block_size)
 
+    own = tiles[:, 0, :]
+    other = lax.ppermute(own, "col", [(0, 1), (1, 0)])
+    row_panel = jnp.where(col_id == 0, jnp.stack([own, other]), jnp.stack([other, own]))
+    row_0, row_1 = from_lead_cols(row_panel)
+
     lead_block = lead_rows_to_all(tiles)
 
-    mine = jnp.stack([tiles[:, 0, :], lead_block[0, :, 0, :], lead_block[1, :, 0, :]])
+    mine = jnp.stack([lead_block[0, :, 0, :], lead_block[1, :, 0, :]])
     other = lax.ppermute(mine, "col", [(0, 1), (1, 0)])
     first, second = jnp.where(col_id == 0, mine, other), jnp.where(col_id == 0, other, mine)
-    payload = jnp.stack([first[0], second[0], first[1], first[2], second[2]])
-    row_0, row_1, m00, m10, m11 = from_lead_cols(payload)
+    m00, m10, m11 = from_lead_cols(jnp.stack([first[0], first[1], second[1]]))
 
     lead_matrix = jnp.concatenate(
         [jnp.concatenate([m00, m10.T], axis=1), jnp.concatenate([m10, m11], axis=1)], axis=0
     )
-    factor = jnp.linalg.cholesky(lead_matrix)
-    inverse = solve_triangular(factor, jnp.eye(lead, dtype=jnp.float32), lower=True)
+    factor, inverse = blocked_factor(lead_matrix, 128)
 
     right = dot(inverse, lead_block.reshape(lead, cols_local * block_size))
     left = lax.dot_general(

time: 374 us -> 297 us (0.79)
  waiting for transfers between devices: 105 us -> 49.5 us
  blocking collectives: 39.5 us -> 94.3 us
  other arithmetic: 144 us -> 109 us
  local copies, waits for them, and re-layouts: 46.8 us -> 15.3 us
  matrix products: 20.1 us -> 16.3 us
    all_to_all x0 -> x1, blocking collectives: none -> 54.8 us  [lead_rows_to_all(): gathered = lax.all_to_all(send, 'row', 0, 0)]
    all_to_all x1 -> x0, waiting for transfers between devices: 45.4 us -> none  [lead_rows_to_all(): gathered = lax.all_to_all(send, 'row', 0, 0)]
    another operation x19 -> x22, other arithmetic: 127 us -> 94.6 us  [the longest x12 50.3 us: blocked_factor(): diag = jnp.linalg.cholesky(blocks[k][k])]
    another operation x37 -> x9, local copies, waits for them, and re-layouts: 21.5 us -> 2.03 us  [the longest x1 0.84 us: shards(): jnp.stack([own, other])]
    another operation x13 -> x4, matrix products: 13.6 us -> 1.06 us  [blocked_factor(): inv = solve_triangular(diag, eye, lower=True)]
    ppermute x2 -> x4, waiting for transfers between devices: 59.2 us -> 49.5 us  [from_lead_cols(): got = lax.ppermute(payload, 'col', pairs)]
    unnamed x38 -> x33, local copies, waits for them, and re-layouts: 13.4 us -> 6.6 us
    dot_general x2 -> x18, matrix products: 5.49 us -> 11.8 us  [dot(): return jnp.dot(a, b, precision=HIGHEST)]
  transfers between devices with their start and end apart: 4 -> 6, of which waited for: 2 -> 2; matrix products, arithmetic and copies ran while one was open for 2% -> 5% of each run, Pallas kernels for 0% -> 0%
where the time goes in v2:
time: 297 us; the launch traced here: 294 us
  other arithmetic  109 us (37%)
  blocking collectives  94.3 us (32%)
  waiting for transfers between devices  49.5 us (17%)
  matrix products  16.3 us (5%)
  local copies, waits for them, and re-layouts  15.3 us (5%)
  starting transfers between devices  8.53 us (3%)
    all_to_all x1, blocking collectives, lead_rows_to_all(): gathered = lax.all_to_all(send, 'row', 0, 0)  54.8 us
    another operation x12, other arithmetic, blocked_factor(): diag = jnp.linalg.cholesky(blocks[k][k])  50.3 us
    ppermute x4, waiting for transfers between devices, from_lead_cols(): got = lax.ppermute(payload, 'col', pairs)  49.5 us
    another operation x8, other arithmetic, blocked_factor(): inv = solve_triangular(diag, eye, lower=True)  42.5 us
    all_to_all x1, blocking collectives, lead_rows_to_all(): spread = lax.all_to_all(send, 'row', 0, 0)[:PANELS]  39.5 us
    dot_general x18, matrix products, dot(): return jnp.dot(a, b, precision=HIGHEST)  11.8 us
    unnamed x33, local copies, waits for them, and re-layouts  6.6 us
    select_n x4, other arithmetic, from_lead_cols(): payload = jnp.where(fresh, got, payload)  6.38 us
  transfers between devices with their start and end apart: 6, of which 2 were waited for; matrix products, arithmetic and copies ran while one was open for 5% of the time, Pallas kernels for 0%

profile of v2, /device:TPU:26, one launch (start us, length us, event | category | flops | bytes accessed | tf_op | source)
XLA Modules:
  0.0 293.5 jit_solution(9696849458454341124)
XLA Ops:
  0.0 1.5 copy.97
  1.5 39.5 %all_to_all.10 = f32[32,8,4,256]{3,2,1,0:T(4,128)S(1)} all-to-all(f32[32,8,4,256]{3,2,1,0:T(4,128)S(1)} %bitcast.111), channel_id=1, replica_groups=mesh['row'=32,'col'=8] {'row'}, dimensions={0} | all-to-all | bytes 2097152 | tf_op jit(solution)/shard_map/all_to_all | solution.py:20
  41.5 54.8 %all_to_all.11 = f32[32,2,8,4,256]{4,3,2,1,0:T(4,128)S(1)} all-to-all(f32[32,2,8,4,256]{4,3,2,1,0:T(4,128)S(1)} %broadcast_in_dim.16), channel_id=1, replica_groups=mesh['row'=32,'col'=8] {'row'}, dimensions={0} | all-to-all | bytes 4194304 | tf_op jit(solution)/shard_map/all_to_all | solution.py:22
  98.3 1.4 collective-permute-start
  101.8 1.3 collective-permute-start.3
  103.2 1.2 broadcast_select_fusion.5
  104.4 1.2 fusion.7
  106.5 1.6 collective-permute-start.1
  108.1 1.9 maximum_select_fusion
  110.0 1.5 collective-permute-start.4
  111.4 1.9 broadcast_select_fusion.3
  113.3 1.3 collective-permute-start.5
  114.6 2.1 broadcast_select_fusion.1
  116.8 1.5 collective-permute-start.2
  118.2 38.5 %collective-permute-done.5 = f32[2,256,256]{2,1,0:T(8,128)} collective-permute-done((f32[2,256,256]{2,1,0:T(8,128)}, f32[2,256,256]{2,1,0:T(8,128)}, u32[]{:S(2)}, u32[]{:S(2)}) %collective-permute-start.5) | collective-permute-done | bytes 524320 | tf_op jit(solution)/shard_map/ppermute | solution.py:32
  159.0 1.8 copy.104
  160.8 11.0 %collective-permute-done.2 = f32[3,256,256]{2,1,0:T(8,128)} collective-permute-done((f32[3,256,256]{2,1,0:T(8,128)}, f32[3,256,256]{2,1,0:T(8,128)}, u32[]{:S(2)}, u32[]{:S(2)}) %collective-permute-start.2) | collective-permute-done | bytes 786464 | tf_op jit(solution)/shard_map/ppermute | solution.py:32
  171.7 1.2 broadcast_select_fusion.2
  173.2 11.7 %cholesky.74 = f32[128,128]{1,0:T(8,128)S(1)} custom-call(f32[128,128]{1,0:T(8,128)S(1)} %copy.62), custom_call_target="Cholesky" | custom-call | tf_op jit(solution)/shard_map/jit(cholesky)/cholesky | solution.py:46
  186.3 9.8 %custom-call.8 = f32[1,128,128]{1,2,0:T(8,128)S(1)} custom-call(f32[1,128,128]{2,1,0:T(8,128)S(1)} %get-tuple-element.26), custom_call_target="InvertDiagBlocksLowerTriangular" | custom-call | tf_op jit(solution)/shard_map/jit(_solve_triangular)/triangular_solve | solution.py:47
  198.6 11.9 %cholesky.85 = f32[128,128]{1,0:T(8,128)S(1)} custom-call(f32[128,128]{1,0:T(8,128)S(1)} %copy.65), custom_call_target="Cholesky" | custom-call | tf_op jit(solution)/shard_map/jit(cholesky)/cholesky | solution.py:46
  211.9 9.8 %custom-call.9 = f32[1,128,128]{1,2,0:T(8,128)S(1)} custom-call(f32[1,128,128]{2,1,0:T(8,128)S(1)} %get-tuple-element.24), custom_call_target="InvertDiagBlocksLowerTriangular" | custom-call | tf_op jit(solution)/shard_map/jit(_solve_triangular)/triangular_solve | solution.py:47
  223.5 11.7 %cholesky.96 = f32[128,128]{1,0:T(8,128)S(1)} custom-call(f32[128,128]{1,0:T(8,128)S(1)} %copy.69), custom_call_target="Cholesky" | custom-call | tf_op jit(solution)/shard_map/jit(cholesky)/cholesky | solution.py:46
  236.0 1.3 select_bitcast_fusion.1
  237.3 9.8 %custom-call.10 = f32[1,128,128]{1,2,0:T(8,128)S(1)} custom-call(f32[1,128,128]{2,1,0:T(8,128)S(1)} %get-tuple-element.22), custom_call_target="InvertDiagBlocksLowerTriangular" | custom-call | tf_op jit(solution)/shard_map/jit(_solve_triangular)/triangular_solve | solution.py:47
  250.1 12.1 %cholesky.107 = f32[128,128]{1,0:T(8,128)S(1)} custom-call(f32[128,128]{1,0:T(8,128)S(1)} %copy.73), custom_call_target="Cholesky" | custom-call | tf_op jit(solution)/shard_map/jit(cholesky)/cholesky | solution.py:46
  263.6 9.8 %custom-call.11 = f32[1,128,128]{1,2,0:T(8,128)S(1)} custom-call(f32[1,128,128]{2,1,0:T(8,128)S(1)} %get-tuple-element.20), custom_call_target="InvertDiagBlocksLowerTriangular" | custom-call | tf_op jit(solution)/shard_map/jit(_solve_triangular)/triangular_solve | solution.py:47
  276.1 5.2 %fusion.51 = f32[512,1024]{1,0:T(8,128)S(1)} fusion(f32[512,1024]{1,0:T(8,128)} %bitcast.115, f32[128,128]{1,0:T(8,128)S(1)} %copy.85, f32[128,128]{1,0:T(8,128)S(1)} %convolution_negate_fusion, f32[128,128]{1,0:T(8,128)S(1)} %convolution_negate_fusion.1, f32[128,128]{1,0:T(8,128)S(1)} %convolution_negate_fusion.2, f32[128,128]{1,0:T(8,128)S(1)} %cholesky.75, ...), kind=kOutput, calls=%fused_computation.121 | convolution fusion | flops 3225157632 | bytes 4915200 | tf_op jit(solution)/shard_map/dot_general | solution.py:12
  283.2 2.1 fusion.58
  285.3 1.3 copy.88
  286.6 1.2 reshape.63
  289.0 2.3 broadcast_select_fusion
  (109 shorter events, 27.3 us)
Async XLA Ops:
  96.7 3.0 %copy-start = (f32[1,1,256,4,1,256]{5,4,3,2,1,0:T(1,128)S(1)}, f32[1,1,256,4,1,256]{5,4,3,2,1,0:T(1,128)}, u32[]{:S(2)}) copy-start(f32[1,1,256,4,1,256]{5,4,3,2,1,0:T(1,128)} %param.22) | copy-start | bytes 3145732
  96.8 0.7 copy-start.2
  98.3 4.8 %collective-permute-start = (f32[2,256,256]{2,1,0:T(8,128)}, f32[2,256,256]{2,1,0:T(8,128)}, u32[]{:S(2)}, u32[]{:S(2)}) collective-permute-start(f32[2,256,256]{2,1,0:T(8,128)} %pad_maximum_fusion.3), channel_id=1, source_target_pairs={{0,1},{1,0},{8,9},{9,8},{16,17},{17,16},{24,25},{25,24},{32,33},{3... | collective-permute-start | bytes 1572872 | tf_op jit(solution)/shard_map/ppermute | solution.py:88
  100.0 1.0 copy-start.3
  101.8 6.3 %collective-permute-start.3 = (f32[256,256]{1,0:T(8,128)}, f32[256,256]{1,0:T(8,128)}, u32[]{:S(2)}, u32[]{:S(2)}) collective-permute-start(f32[256,256]{1,0:T(8,128)} %get-tuple-element.31), channel_id=1, source_target_pairs={{0,1},{1,0},{8,9},{9,8},{16,17},{17,16},{24,25},{25,24},{32,33},{3... | collective-permute-start | bytes 786440 | tf_op jit(solution)/shard_map/ppermute | solution.py:81
  103.1 4.9 %copy-start.4 = (f32[1,256,256]{2,1,0:T(8,128)S(1)}, f32[1,256,256]{2,1,0:T(8,128)}, u32[]{:S(2)}) copy-start(f32[1,256,256]{2,1,0:T(8,128)} %get-tuple-element.30) | copy-start | bytes 786436
  104.4 1.2 copy-start.1
  105.6 4.4 %copy-start.6 = (f32[1,256,256]{2,1,0:T(8,128)}, f32[1,256,256]{2,1,0:T(8,128)S(1)}, u32[]{:S(2)}) copy-start(f32[1,256,256]{2,1,0:T(8,128)S(1)} %fusion.7) | copy-start | bytes 786436
  105.6 5.8 %copy-start.5 = (f32[1,256,256]{2,1,0:T(8,128)S(1)}, f32[1,256,256]{2,1,0:T(8,128)}, u32[]{:S(2)}) copy-start(f32[1,256,256]{2,1,0:T(8,128)} %get-tuple-element.30) | copy-start | bytes 786436
  106.5 8.1 %collective-permute-start.1 = (f32[3,256,256]{2,1,0:T(8,128)}, f32[3,256,256]{2,1,0:T(8,128)}, u32[]{:S(2)}, u32[]{:S(2)}) collective-permute-start(f32[3,256,256]{2,1,0:T(8,128)} %pad_maximum_fusion), channel_id=1, source_target_pairs={{0,2},{1,3},{8,10},{9,11},{16,18},{17,19},{24,26},{25,27},{32,34},... | collective-permute-start | bytes 2359304 | tf_op jit(solution)/shard_map/ppermute | solution.py:32
  110.0 1.5 collective-permute-start.4
  113.3 43.4 %collective-permute-start.5 = (f32[2,256,256]{2,1,0:T(8,128)}, f32[2,256,256]{2,1,0:T(8,128)}, u32[]{:S(2)}, u32[]{:S(2)}) collective-permute-start(f32[2,256,256]{2,1,0:T(8,128)} %broadcast_select_fusion.3), channel_id=1, source_target_pairs={{0,4},{1,5},{2,6},{3,7},{8,12},{9,13},{10,14},{11,15},{16,20},{17,... | collective-permute-start | bytes 1572872 | tf_op jit(solution)/shard_map/ppermute | solution.py:32
  116.8 55.0 %collective-permute-start.2 = (f32[3,256,256]{2,1,0:T(8,128)}, f32[3,256,256]{2,1,0:T(8,128)}, u32[]{:S(2)}, u32[]{:S(2)}) collective-permute-start(f32[3,256,256]{2,1,0:T(8,128)} %broadcast_select_fusion.1), channel_id=1, source_target_pairs={{0,4},{1,5},{2,6},{3,7},{8,12},{9,13},{10,14},{11,15},{16,20},{17,... | collective-permute-start | bytes 2359304 | tf_op jit(solution)/shard_map/ppermute | solution.py:32
  276.1 5.2 %copy-start.9 = (f32[256,256]{1,0:T(8,128)S(1)}, f32[256,256]{1,0:T(8,128)}, u32[]{:S(2)}) copy-start(f32[256,256]{1,0:T(8,128)} %get-tuple-element.39) | copy-start | bytes 786436
  276.1 5.2 %copy-start.10 = (f32[128,128]{1,0:T(8,128)S(1)}, f32[128,128]{1,0:T(8,128)}, u32[]{:S(2)}) copy-start(f32[128,128]{1,0:T(8,128)} %get-tuple-element.23) | copy-start | bytes 196612
  282.4 0.8 copy-start.7
  287.8 3.5 %copy-start.8 = (f32[256,512]{1,0:T(8,128)S(1)}, f32[256,512]{1,0:T(8,128)}, u32[]{:S(2)}) copy-start(f32[256,512]{1,0:T(8,128)} %copy-done.7) | copy-start | bytes 1572868
